TPU v7x, 32 devices: a whole 2x2x4 slice. The times are simulated.
32 devices in a mesh: row: 4 (over x, core), col: 8 (over z, y).
Axes of the slice: x: 2, y: 2, z: 4, core: 2. Of those that a mesh axis runs over, the one named last changes fastest.
Arguments:
- embed: bfloat16 [1024, 768], P(('row', 'col'))
- beta: bfloat16 [1024], P(('row', 'col')), may hold values from 16 to 400
- block_mask: int32 [8, 8], P('row'), may hold values from 0 to 1, as said below
- counts: int32 [8], replicated, may hold values from 2 to 128
- probes: float32 [64, 1024], P(None, ('row', 'col')), may hold values from -6 to 6
Outputs:
- spectral: float32 [64, 1024], P(None, ('row', 'col'))
Inputs may be any that keep to these rules, and one draw needn't show every extreme that they name: `block_mask`: every diagonal entry is 1.
All inputs are finite; a program needn't handle non-finite values.
Results may differ from a plain program's by a relative error of at most 0.012.
The roundings to bfloat16 on the way count: a program that leaves them out, or rounds other values in their place, can miss the bound.
Values may be sent and summed in bfloat16 or wider, within the bound.
No kernel may reach another device: no remote copies, remote signals or barrier semaphores. Data moves between devices by JAX's collectives and lax.ppermute only.
A program may use at most 64 MiB of HBM per device.

v0:
```python
import jax
import jax.numpy as jnp
from jax import lax
from jax.sharding import PartitionSpec as P

ITERS = 2


def spread(shard, axis, root):
    mine = lax.axis_index(axis) == root
    return lax.psum(jnp.where(mine, shard, jnp.zeros_like(shard)), axis)


def own_piece(totals, col_ratio, n_row, row_index, col_index):
    shard_len = totals.shape[1] // n_row
    chosen = jnp.zeros_like(totals)
    for root_k in range(col_ratio):
        received = spread(totals, "col", col_ratio * row_index + root_k)
        chosen = jnp.where(col_index // n_row == root_k, received, chosen)
    return lax.dynamic_slice_in_dim(chosen, col_index % n_row * shard_len, shard_len, 1)


def body(embed, beta, block_mask, counts, probes):
    n_row = lax.axis_size("row")
    n_col = lax.axis_size("col")
    col_ratio = n_col // n_row
    row_index = lax.axis_index("row")
    col_index = lax.axis_index("col")
    shard_len, feat_width = embed.shape
    row_files = shard_len * n_col
    col_files = shard_len * n_row
    values = embed.astype(jnp.float32)
    unit_vec = (
        values * lax.rsqrt(jnp.mean(values * values, axis=1, keepdims=True) + 1e-06)
    ).astype(jnp.bfloat16)
    unit_rows, beta_rows = (
        lax.all_gather(unit_vec, "col", axis=0, tiled=True),
        lax.all_gather(beta, "col", axis=0, tiled=True),
    )
    half_pick = col_index % col_ratio
    col_seq = lax.iota(jnp.int32, col_files)
    unit_cols = spread(
        lax.dynamic_slice_in_dim(unit_rows, half_pick * col_files, col_files, 0),
        "row",
        col_index // col_ratio,
    )
    col_ids = col_index * col_files + col_seq
    gram_tile = lax.dot_general(
        unit_rows, unit_cols, (((1,), (1,)), ((), ())), preferred_element_type=jnp.float32
    )
    scores = gram_tile * (beta_rows.astype(jnp.float32) / feat_width)[:, None]
    row_blocks = block_mask.shape[0]
    blk_size = row_files // row_blocks
    col_block = col_ids // blk_size
    col_live = col_ids % blk_size < jnp.take(counts, col_block, axis=0)
    mask_cols = jnp.take(block_mask, col_block, axis=1) == 1
    block_wide = jnp.broadcast_to(mask_cols[:, None, :], (row_blocks, blk_size, col_files)).reshape(
        row_files, col_files
    )
    row_ids = row_index * row_files + lax.iota(jnp.int32, row_files)
    allowed = block_wide & col_live[None, :] & (row_ids[:, None] != col_ids[None, :])
    masked = jnp.where(allowed, scores, -1e30)
    local_top = jnp.max(masked, axis=1)
    row_top = lax.pmax(local_top, "col")
    row_mass = lax.psum(
        jnp.sum(jnp.where(allowed, jnp.exp(masked - row_top[:, None]), 0.0), axis=1), "col"
    )
    weights = jnp.where(allowed, jnp.exp(masked - row_top[:, None]) / row_mass[:, None], 0.0)
    col_mass = lax.psum(jnp.sum(weights, axis=0), "row")
    own_mass = own_piece(col_mass[None, :], col_ratio, n_row, row_index, col_index)[0]
    inv_root = lax.rsqrt((1.0 + own_mass) * 0.5)
    affinity = weights.astype(jnp.bfloat16)
    probe_state = probes
    for sweep in range(ITERS):
        scaled = (probe_state * inv_root[None, :]).astype(jnp.bfloat16)
        probe_rows = lax.all_gather(scaled, "col", axis=1, tiled=True)
        probe_cols = spread(
            lax.dynamic_slice_in_dim(probe_rows, half_pick * col_files, col_files, 1),
            "row",
            col_index // col_ratio,
        )
        row_part = lax.dot_general(
            probe_cols, affinity, (((1,), (1,)), ((), ())), preferred_element_type=jnp.float32
        )
        col_part = jnp.dot(probe_rows, affinity, preferred_element_type=jnp.float32)
        own_rows = lax.psum_scatter(
            row_part.astype(jnp.bfloat16), "col", scatter_dimension=1, tiled=True
        ).astype(jnp.float32)
        col_total = lax.psum(col_part, "row")
        own_cols = own_piece(col_total, col_ratio, n_row, row_index, col_index)
        probe_state = (own_rows + own_cols) * (0.5 * inv_root)[None, :]
    return probe_state


def solution(mesh):
    placed = (
        P(("row", "col"), None),
        P(("row", "col")),
        P("row", None),
        P(),
        P(None, ("row", "col")),
    )
    return jax.shard_map(
        body, mesh=mesh, in_specs=placed, out_specs=P(None, ("row", "col")), check_vma=False
    )
```

profile of v0, /device:TPU:0, one launch (start us, length us, event | category | flops | bytes accessed | tf_op | source)
XLA Modules:
  0.0 495.1 jit_solution(6957773946014642195)
XLA Ops:
  6.5 0.0 copy-start
  6.5 0.0 all-reduce.8.cloned.1.call-start
  6.5 0.8 copy-done
  7.3 0.1 fusion.1
  7.5 0.1 fusion.2
  7.5 32.7 %all_gather.12 = bf16[256,768]{1,0:T(8,128)(2,1)S(1)} all-gather(bf16[32,768]{1,0:T(8,128)(2,1)S(1)} %fusion.2), channel_id=1, replica_groups=mesh['row'=4,'col'=8] {'col'}, dimensions={0}, use_global_device_ids=true | all-gather | bytes 442368 | tf_op jit(solution)/shard_map/all_gather | solution.py:37
  40.3 0.7 dynamic-slice_select_fusion
  41.0 0.0 all-reduce.8.cloned.1.call-update
  41.0 0.0 reduce-scatter.3.cloned.1.call-start
  41.2 0.0 copy-start.1
  41.2 0.6 copy-done.1
  41.8 0.7 fusion.21
  42.5 0.0 copy-start.3
  42.5 0.7 copy-done.3
  43.2 0.1 copy.9
  43.3 0.6 gather_fusion
  43.9 0.1 fusion.3
  44.0 0.1 copy.10
  44.1 0.1 copy.11
  44.2 0.0 copy-start.5
  44.3 0.6 copy-done.5
  44.9 0.6 dynamic-slice
  46.1 0.0 copy-start.4
  46.2 0.6 copy-done.4
  46.8 0.2 dynamic-update-slice
  47.0 21.5 %all-reduce = bf16[256]{0:T(256)(128)(2,1)S(1)} all-reduce(bf16[256]{0:T(256)(128)(2,1)S(1)} %dynamic-update-slice), channel_id=1, replica_groups=mesh['row'=4,'col'=8] {'col'}, use_global_device_ids=true, to_apply=%add | all-reduce | flops 256 | bytes 1024
  68.5 5.1 %fusion.12 = pred[128]{0:T(512)(128)(4,1)S(1)} fusion(s32[]{:T(128)} %bitcast.3, s32[]{:T(128)} %bitcast.4, s32[]{:T(128)} %bitcast.5, s32[]{:T(128)} %bitcast.6, s32[]{:T(128)} %bitcast.7, s32[]{:T(128)} %bitcast.8, s32[]{:T(128)} %bitcast.9, s32[]{:T(128)} %bitcast.10, s32[]{:T(128)S(6)} %mul.86), kind=kLoop, calls=%fused_computation.62 | loop fusion | flops 7808 | bytes 164 | tf_op jit(solution)/shard_map/lt | solution.py:55
  73.6 0.4 all-reduce.8.cloned.1.call-done
  74.0 1.2 fusion.22
  75.2 21.3 %pmax.7 = f32[256]{0:T(256)S(1)} all-reduce(f32[256]{0:T(256)S(1)} %get-tuple-element.29), channel_id=1, replica_groups=mesh['row'=4,'col'=8] {'col'}, use_global_device_ids=true, to_apply=%region_3.4 | all-reduce | flops 256 | bytes 2048 | tf_op jit(solution)/shard_map/pmax | solution.py:64
  96.6 0.1 select_reduce_fusion
  96.7 17.1 %psum.92 = f32[256]{0:T(256)S(1)} all-reduce(f32[256]{0:T(256)S(1)} %select_reduce_fusion), channel_id=1, replica_groups=mesh['row'=4,'col'=8] {'col'}, use_global_device_ids=true, to_apply=%region_5.6 | all-reduce | flops 256 | bytes 2048 | tf_op jit(solution)/shard_map/psum | solution.py:65
  113.8 0.2 fusion.11
  114.0 0.0 copy-start.2
  114.0 5.9 %psum.93 = f32[128]{0:T(128)S(1)} all-reduce(f32[128]{0:T(128)S(1)} %get-tuple-element.13), channel_id=1, replica_groups=mesh['row'=4,'col'=8] {'row'}, use_global_device_ids=true, to_apply=%region_7.8 | all-reduce | flops 128 | bytes 1024 | tf_op jit(solution)/shard_map/psum | solution.py:69
  119.9 19.1 %all-reduce.3 = (f32[1,128]{1,0:T(1,128)S(1)}, f32[1,128]{1,0:T(1,128)S(1)}) all-reduce(f32[1,128]{1,0:T(1,128)S(1)} %get-tuple-element.20, f32[1,128]{1,0:T(1,128)S(1)} %get-tuple-element.19), channel_id=1, replica_groups=mesh['row'=4,'col'=8] {'col'}, use_global_device_ids=true, to_apply=%region_8.9 | all-reduce | flops 256 | bytes 2048 | tf_op jit(solution)/shard_map/psum | solution.py:11
  139.0 0.1 multiply_bitcast_fusion
  139.1 0.0 copy-done.2
  139.1 0.1 multiply_convert_fusion
  139.2 30.5 %all_gather.14 = bf16[64,256]{0,1:T(8,128)(2,1)S(1)} all-gather(bf16[64,32]{0,1:T(8,128)(2,1)S(1)} %multiply_convert_fusion), channel_id=1, replica_groups=mesh['row'=4,'col'=8] {'col'}, dimensions={1}, use_global_device_ids=true | all-gather | bytes 36864 | tf_op jit(solution)/shard_map/all_gather | solution.py:76
  169.7 10.3 %psum.96 = bf16[64,128]{0,1:T(8,128)(2,1)S(1)} all-reduce(bf16[64,128]{0,1:T(8,128)(2,1)S(1)} %dynamic-slice_select_fusion.2), channel_id=1, replica_groups=mesh['row'=4,'col'=8] {'row'}, use_global_device_ids=true, to_apply=%region_10.11 | all-reduce | flops 8192 | bytes 32768 | tf_op jit(solution)/shard_map/psum | solution.py:11
  180.0 0.1 fusion.23
  180.1 0.8 convolution_convert_fusion.1
  181.0 0.0 reduce-scatter.3.cloned.1.call-update
  181.0 0.0 all-reduce.12.cloned.1.call-start
  181.0 10.7 %psum.97 = f32[64,128]{0,1:T(8,128)S(1)} all-reduce(f32[64,128]{0,1:T(8,128)S(1)} %fusion.23), channel_id=1, replica_groups=mesh['row'=4,'col'=8] {'row'}, use_global_device_ids=true, to_apply=%region_12.13 | all-reduce | flops 8192 | bytes 65536 | tf_op jit(solution)/shard_map/psum | solution.py:89
  191.8 0.7 broadcast_select_fusion.2
  192.4 0.0 all-reduce.12.cloned.1.call-update
  192.4 0.0 reduce-scatter.5.cloned.1.call-start
  192.5 46.2 %reduce-scatter.3.cloned.1.call-done = bf16[64,32]{0,1:T(8,128)(2,1)} async-done(((bf16[64,256]{0,1:T(8,128)(2,1)}), bf16[64,32]{0,1:T(8,128)(2,1)}) %reduce-scatter.3.cloned.1.call-update) | async-done | bytes 4112 | tf_op jit(solution)/shard_map/reduce_scatter | solution.py:86
  238.7 72.8 %all-reduce.12.cloned.1.call-done = (f32[64,128]{0,1:T(8,128)}, f32[64,128]{0,1:T(8,128)}) async-done(((f32[64,128]{0,1:T(8,128)}, f32[64,128]{0,1:T(8,128)}), (f32[64,128]{0,1:T(8,128)}, f32[64,128]{0,1:T(8,128)})) %all-reduce.12.cloned.1.call-update) | async-done | bytes 65552 | tf_op jit(solution)/shard_map/psum | solution.py:11
  311.5 0.8 fusion.9
  312.3 30.5 %all_gather.15 = bf16[64,256]{0,1:T(8,128)(2,1)S(1)} all-gather(bf16[64,32]{0,1:T(8,128)(2,1)S(1)} %fusion.9), channel_id=1, replica_groups=mesh['row'=4,'col'=8] {'col'}, dimensions={1}, use_global_device_ids=true | all-gather | bytes 36864 | tf_op jit(solution)/shard_map/all_gather | solution.py:76
  342.8 0.1 fusion.24
  343.0 10.3 %psum.100 = bf16[64,128]{0,1:T(8,128)(2,1)S(1)} all-reduce(bf16[64,128]{0,1:T(8,128)(2,1)S(1)} %dynamic-slice_select_fusion.1), channel_id=1, replica_groups=mesh['row'=4,'col'=8] {'row'}, use_global_device_ids=true, to_apply=%region_15.16 | all-reduce | flops 8192 | bytes 32768 | tf_op jit(solution)/shard_map/psum | solution.py:11
  353.3 0.8 convolution_convert_fusion
  354.1 0.0 reduce-scatter.5.cloned.1.call-update
  354.1 0.0 all-reduce.10.cloned.1.call-start
  354.2 11.8 %psum.101 = f32[64,128]{0,1:T(8,128)S(1)} all-reduce(f32[64,128]{0,1:T(8,128)S(1)} %fusion.24), channel_id=1, replica_groups=mesh['row'=4,'col'=8] {'row'}, use_global_device_ids=true, to_apply=%region_17.18 | all-reduce | flops 8192 | bytes 65536 | tf_op jit(solution)/shard_map/psum | solution.py:89
  366.0 0.7 broadcast_select_fusion.1
  366.6 0.0 all-reduce.10.cloned.1.call-update
  366.7 48.3 %reduce-scatter.5.cloned.1.call-done = bf16[64,32]{0,1:T(8,128)(2,1)} async-done(((bf16[64,256]{0,1:T(8,128)(2,1)}), bf16[64,32]{0,1:T(8,128)(2,1)}) %reduce-scatter.5.cloned.1.call-update) | async-done | bytes 4112 | tf_op jit(solution)/shard_map/reduce_scatter | solution.py:86
  415.0 72.3 %all-reduce.10.cloned.1.call-done = (f32[64,128]{0,1:T(8,128)}, f32[64,128]{0,1:T(8,128)}) async-done(((f32[64,128]{0,1:T(8,128)}, f32[64,128]{0,1:T(8,128)}), (f32[64,128]{0,1:T(8,128)}, f32[64,128]{0,1:T(8,128)})) %all-reduce.10.cloned.1.call-update) | async-done | bytes 65552 | tf_op jit(solution)/shard_map/psum | solution.py:11
  487.2 1.4 fusion.5
  (13 shorter events, 0.1 us)
Async XLA Ops:
  6.5 0.8 copy-start
  6.5 67.5 %all-reduce.8.cloned.1.call-start = ((), (), s32[]{:S(2)}) async-start(), calls=%async_computation.2 | async-start | bytes 393216 | tf_op jit(solution)/shard_map/psum | solution.py:11
  41.0 197.7 %reduce-scatter.3.cloned.1.call-start = ((), (), s32[]{:S(2)}) async-start(), calls=%async_computation.3 | async-start | bytes 73728 | tf_op jit(solution)/shard_map/reduce_scatter | solution.py:86
  41.2 0.7 copy-start.1
  42.5 0.7 copy-start.3
  44.2 0.7 copy-start.5
  46.1 0.7 copy-start.4
  114.0 25.1 %copy-start.2 = (f32[64,32]{0,1:T(8,128)S(1)}, f32[64,32]{0,1:T(8,128)}, u32[]{:S(2)}) copy-start(f32[64,32]{0,1:T(8,128)} %param.9) | copy-start | bytes 24580
  181.0 130.5 %all-reduce.12.cloned.1.call-start = ((), (), s32[]{:S(2)}) async-start(), calls=%async_computation.6 | async-start | bytes 262144 | tf_op jit(solution)/shard_map/psum | solution.py:11
  192.4 222.5 %reduce-scatter.5.cloned.1.call-start = ((), (), s32[]{:S(2)}) async-start(), calls=%async_computation.4 | async-start | bytes 73728 | tf_op jit(solution)/shard_map/reduce_scatter | solution.py:86
  354.1 133.1 %all-reduce.10.cloned.1.call-start = ((), (), s32[]{:S(2)}) async-start(), calls=%async_computation.5 | async-start | bytes 262144 | tf_op jit(solution)/shard_map/psum | solution.py:11
Sparse Core Ops, SparseCore 0:
  41.1 32.8 all-reduce.7
  181.1 57.5 reduce-scatter.2
  242.6 68.8 all-reduce.11
  354.3 60.6 reduce-scatter.4
  418.3 68.8 all-reduce.9
where the time goes:
time: 496 us; the launch traced here: 495 us
  waiting for transfers between devices  240 us (48%)
  blocking collectives  222 us (45%)
  between operations  14 us (3%)
  other arithmetic  10.2 us (2%)
  local copies, waits for them, and re-layouts  5.8 us (1%)
    psum x3, waiting for transfers between devices, spread(): return lax.psum(jnp.where(mine, shard, jnp.zeros_like(shard)), axis)  145 us
    reduce_scatter x2, waiting for transfers between devices, body(): lax.psum_scatter(row_part.astype(jnp.bfloat16), 'col', scatter_dimension=...  94.5 us
    all_gather x2, blocking collectives, body(): probe_rows = lax.all_gather(scaled, 'col', axis=1, tiled=True)  61 us
    psum x3, blocking collectives, spread(): return lax.psum(jnp.where(mine, shard, jnp.zeros_like(shard)), axis)  39.7 us
    all_gather x1, blocking collectives, body(): lax.all_gather(unit_vec, 'col', axis=0, tiled=True)  32.7 us
    psum x2, blocking collectives, body(): col_total = lax.psum(col_part, 'row')  22.5 us
    unnamed x1, blocking collectives  21.5 us
    pmax x1, blocking collectives, body(): row_top = lax.pmax(local_top, 'col')  21.3 us
  transfers between devices with their start and end apart: 5, of which 5 were waited for; matrix products, arithmetic and copies ran while one was open for 2% of the time, Pallas kernels for 0%

commit v1 on v0

--- a/solution.py
+++ b/solution.py
@@ -73,7 +73,15 @@
     probe_state = probes
     for sweep in range(ITERS):
         scaled = (probe_state * inv_root[None, :]).astype(jnp.bfloat16)
-        probe_rows = lax.all_gather(scaled, "col", axis=1, tiled=True)
+        ways, here = (lax.axis_size("col"), lax.axis_index("col"))
+        grown, reach = (scaled, 1)
+        while reach < ways:
+            theirs = lax.ppermute(grown, "col", [(d, d ^ reach) for d in range(ways)])
+            mine_first = jnp.concatenate([grown, theirs], axis=1)
+            theirs_first = jnp.concatenate([theirs, grown], axis=1)
+            grown = jnp.where(here & reach == 0, mine_first, theirs_first)
+            reach = 2 * reach
+        probe_rows = grown
         probe_cols = spread(
             lax.dynamic_slice_in_dim(probe_rows, half_pick * col_files, col_files, 1),
             "row",

time: 496 us -> 460 us (0.927)
  blocking collectives: 222 us -> 160 us
  waiting for transfers between devices: 240 us -> 261 us
    all_gather x2 -> x0, blocking collectives: 61 us -> none  [body(): probe_rows = lax.all_gather(scaled, 'col', axis=1, tiled=True)]
    ppermute x0 -> x6, waiting for transfers between devices: none -> 20.9 us  [body(): theirs = lax.ppermute(grown, 'col', [(d, d ^ reach) for d in range(ways)])]
  transfers between devices with their start and end apart: 5 -> 11, of which waited for: 5 -> 11; matrix products, arithmetic and copies ran while one was open for 2% -> 2% of each run, Pallas kernels for 0% -> 0%
where the time goes in v1:
time: 460 us; the launch traced here: 459 us
  waiting for transfers between devices  261 us (57%)
  blocking collectives  160 us (35%)
  between operations  14.1 us (3%)
  other arithmetic  10.3 us (2%)
  local copies, waits for them, and re-layouts  5.8 us (1%)
    psum x3, waiting for transfers between devices, spread(): return lax.psum(jnp.where(mine, shard, jnp.zeros_like(shard)), axis)  145 us
    reduce_scatter x2, waiting for transfers between devices, body(): lax.psum_scatter(row_part.astype(jnp.bfloat16), 'col', scatter_dimension=...  95 us
    psum x3, blocking collectives, spread(): return lax.psum(jnp.where(mine, shard, jnp.zeros_like(shard)), axis)  39.7 us
    all_gather x1, blocking collectives, body(): lax.all_gather(unit_vec, 'col', axis=0, tiled=True)  32.7 us
    psum x2, blocking collectives, body(): col_total = lax.psum(col_part, 'row')  22.1 us
    unnamed x1, blocking collectives  21.5 us
    pmax x1, blocking collectives, body(): row_top = lax.pmax(local_top, 'col')  21.3 us
    ppermute x6, waiting for transfers between devices, body(): theirs = lax.ppermute(grown, 'col', [(d, d ^ reach) for d in range(ways)])  20.9 us
  transfers between devices with their start and end apart: 11, of which 11 were waited for; matrix products, arithmetic and copies ran while one was open for 2% of the time, Pallas kernels for 0%

profile of v1, /device:TPU:0, one launch (start us, length us, event | category | flops | bytes accessed | tf_op | source)
XLA Modules:
  0.0 459.0 jit_solution(12735307957406408422)
XLA Ops:
  6.5 0.8 copy-done
  7.3 0.1 fusion.1
  7.5 0.1 fusion.2
  7.5 32.7 %all_gather.6 = bf16[256,768]{1,0:T(8,128)(2,1)S(1)} all-gather(bf16[32,768]{1,0:T(8,128)(2,1)S(1)} %fusion.2), channel_id=1, replica_groups=mesh['row'=4,'col'=8] {'col'}, dimensions={0}, use_global_device_ids=true | all-gather | bytes 442368 | tf_op jit(solution)/shard_map/all_gather | solution.py:37
  40.3 0.7 dynamic-slice_select_fusion
  41.0 0.0 all-reduce.8.cloned.1.call-update
  41.0 0.0 reduce-scatter.3.cloned.1.call-start
  41.2 0.6 copy-done.1
  41.8 0.7 fusion.21
  42.5 0.7 copy-done.3
  43.2 0.1 copy.9
  43.3 0.6 gather_fusion
  43.9 0.1 fusion.3
  44.0 0.1 copy.10
  44.1 0.1 copy.11
  44.3 0.6 copy-done.5
  44.9 0.6 dynamic-slice
  46.2 0.6 copy-done.4
  46.8 0.2 dynamic-update-slice
  47.0 21.5 %all-reduce = bf16[256]{0:T(256)(128)(2,1)S(1)} all-reduce(bf16[256]{0:T(256)(128)(2,1)S(1)} %dynamic-update-slice), channel_id=1, replica_groups=mesh['row'=4,'col'=8] {'col'}, use_global_device_ids=true, to_apply=%add | all-reduce | flops 256 | bytes 1024
  68.5 5.1 %fusion.12 = pred[128]{0:T(512)(128)(4,1)S(1)} fusion(s32[]{:T(128)} %bitcast.3, s32[]{:T(128)} %bitcast.4, s32[]{:T(128)} %bitcast.5, s32[]{:T(128)} %bitcast.6, s32[]{:T(128)} %bitcast.7, s32[]{:T(128)} %bitcast.8, s32[]{:T(128)} %bitcast.9, s32[]{:T(128)} %bitcast.10, s32[]{:T(128)S(6)} %mul.86), kind=kLoop, calls=%fused_computation.68 | loop fusion | flops 7808 | bytes 164 | tf_op jit(solution)/shard_map/lt | solution.py:55
  73.6 0.4 all-reduce.8.cloned.1.call-done
  74.0 1.2 fusion.22
  75.2 21.3 %pmax.7 = f32[256]{0:T(256)S(1)} all-reduce(f32[256]{0:T(256)S(1)} %get-tuple-element.29), channel_id=1, replica_groups=mesh['row'=4,'col'=8] {'col'}, use_global_device_ids=true, to_apply=%region_3.4 | all-reduce | flops 256 | bytes 2048 | tf_op jit(solution)/shard_map/pmax | solution.py:64
  96.6 0.1 select_reduce_fusion
  96.7 17.1 %psum.92 = f32[256]{0:T(256)S(1)} all-reduce(f32[256]{0:T(256)S(1)} %select_reduce_fusion), channel_id=1, replica_groups=mesh['row'=4,'col'=8] {'col'}, use_global_device_ids=true, to_apply=%region_5.6 | all-reduce | flops 256 | bytes 2048 | tf_op jit(solution)/shard_map/psum | solution.py:65
  113.8 0.2 fusion.11
  114.0 5.9 %psum.93 = f32[128]{0:T(128)S(1)} all-reduce(f32[128]{0:T(128)S(1)} %get-tuple-element.13), channel_id=1, replica_groups=mesh['row'=4,'col'=8] {'row'}, use_global_device_ids=true, to_apply=%region_7.8 | all-reduce | flops 128 | bytes 1024 | tf_op jit(solution)/shard_map/psum | solution.py:69
  119.9 19.1 %all-reduce.3 = (f32[1,128]{1,0:T(1,128)S(1)}, f32[1,128]{1,0:T(1,128)S(1)}) all-reduce(f32[1,128]{1,0:T(1,128)S(1)} %get-tuple-element.20, f32[1,128]{1,0:T(1,128)S(1)} %get-tuple-element.19), channel_id=1, replica_groups=mesh['row'=4,'col'=8] {'col'}, use_global_device_ids=true, to_apply=%region_8.9 | all-reduce | flops 256 | bytes 2048 | tf_op jit(solution)/shard_map/psum | solution.py:11
  139.0 0.1 multiply_bitcast_fusion
  139.1 0.1 multiply_convert_fusion
  139.2 3.6 collective-permute-done
  142.9 0.1 collective-permute-start.1
  142.9 3.7 collective-permute-done.1
  146.7 0.1 collective-permute-start.2
  146.8 4.8 %collective-permute-done.2 = bf16[64,128]{0,1:T(8,128)(2,1)S(1)} collective-permute-done((bf16[64,128]{0,1:T(8,128)(2,1)S(1)}, bf16[64,128]{0,1:T(8,128)(2,1)S(1)}, u32[]{:S(2)}, u32[]{:S(2)}) %collective-permute-start.2) | collective-permute-done | bytes 16416 | tf_op jit(solution)/shard_map/ppermute | solution.py:79
  151.6 10.3 %psum.96 = bf16[64,128]{0,1:T(8,128)(2,1)S(1)} all-reduce(bf16[64,128]{0,1:T(8,128)(2,1)S(1)} %dynamic-slice_select_fusion.2), channel_id=1, replica_groups=mesh['row'=4,'col'=8] {'row'}, use_global_device_ids=true, to_apply=%region_10.11 | all-reduce | flops 8192 | bytes 32768 | tf_op jit(solution)/shard_map/psum | solution.py:11
  161.9 0.1 fusion.23
  162.0 0.8 convolution_convert_fusion.1
  162.9 0.0 reduce-scatter.3.cloned.1.call-update
  162.9 0.0 all-reduce.12.cloned.1.call-start
  163.0 10.7 %psum.97 = f32[64,128]{0,1:T(8,128)S(1)} all-reduce(f32[64,128]{0,1:T(8,128)S(1)} %fusion.23), channel_id=1, replica_groups=mesh['row'=4,'col'=8] {'row'}, use_global_device_ids=true, to_apply=%region_12.13 | all-reduce | flops 8192 | bytes 65536 | tf_op jit(solution)/shard_map/psum | solution.py:97
  173.7 0.7 broadcast_select_fusion.2
  174.3 0.0 all-reduce.12.cloned.1.call-update
  174.3 0.0 reduce-scatter.5.cloned.1.call-start
  174.4 46.0 %reduce-scatter.3.cloned.1.call-done = bf16[64,32]{0,1:T(8,128)(2,1)} async-done(((bf16[64,256]{0,1:T(8,128)(2,1)}), bf16[64,32]{0,1:T(8,128)(2,1)}) %reduce-scatter.3.cloned.1.call-update) | async-done | bytes 4112 | tf_op jit(solution)/shard_map/reduce_scatter | solution.py:94
  220.4 72.8 %all-reduce.12.cloned.1.call-done = (f32[64,128]{0,1:T(8,128)}, f32[64,128]{0,1:T(8,128)}) async-done(((f32[64,128]{0,1:T(8,128)}, f32[64,128]{0,1:T(8,128)}), (f32[64,128]{0,1:T(8,128)}, f32[64,128]{0,1:T(8,128)})) %all-reduce.12.cloned.1.call-update) | async-done | bytes 65552 | tf_op jit(solution)/shard_map/psum | solution.py:11
  293.2 0.8 fusion.9
  294.0 0.8 collective-permute-start.3
  294.8 2.9 collective-permute-done.3
  297.7 1.1 collective-permute-start.4
  298.7 2.7 collective-permute-done.4
  301.5 1.8 collective-permute-start.5
  303.3 3.1 collective-permute-done.5
  306.4 0.1 fusion.24
  306.6 10.3 %psum.100 = bf16[64,128]{0,1:T(8,128)(2,1)S(1)} all-reduce(bf16[64,128]{0,1:T(8,128)(2,1)S(1)} %dynamic-slice_select_fusion.1), channel_id=1, replica_groups=mesh['row'=4,'col'=8] {'row'}, use_global_device_ids=true, to_apply=%region_15.16 | all-reduce | flops 8192 | bytes 32768 | tf_op jit(solution)/shard_map/psum | solution.py:11
  316.8 0.8 convolution_convert_fusion
  317.7 0.0 reduce-scatter.5.cloned.1.call-update
  317.7 0.0 all-reduce.10.cloned.1.call-start
  317.8 11.4 %psum.101 = f32[64,128]{0,1:T(8,128)S(1)} all-reduce(f32[64,128]{0,1:T(8,128)S(1)} %fusion.24), channel_id=1, replica_groups=mesh['row'=4,'col'=8] {'row'}, use_global_device_ids=true, to_apply=%region_17.18 | all-reduce | flops 8192 | bytes 65536 | tf_op jit(solution)/shard_map/psum | solution.py:97
  329.2 0.7 broadcast_select_fusion.1
  329.8 49.0 %reduce-scatter.5.cloned.1.call-done = bf16[64,32]{0,1:T(8,128)(2,1)} async-done(((bf16[64,256]{0,1:T(8,128)(2,1)}), bf16[64,32]{0,1:T(8,128)(2,1)}) %reduce-scatter.5.cloned.1.call-update) | async-done | bytes 4112 | tf_op jit(solution)/shard_map/reduce_scatter | solution.py:94
  378.8 72.2 %all-reduce.10.cloned.1.call-done = (f32[64,128]{0,1:T(8,128)}, f32[64,128]{0,1:T(8,128)}) async-done(((f32[64,128]{0,1:T(8,128)}, f32[64,128]{0,1:T(8,128)}), (f32[64,128]{0,1:T(8,128)}, f32[64,128]{0,1:T(8,128)})) %all-reduce.10.cloned.1.call-update) | async-done | bytes 65552 | tf_op jit(solution)/shard_map/psum | solution.py:11
  451.0 1.4 fusion.5
  (29 shorter events, 0.3 us)
Async XLA Ops:
  6.5 0.8 copy-start
  6.5 67.5 %all-reduce.8.cloned.1.call-start = ((), (), s32[]{:S(2)}) async-start(), calls=%async_computation.2 | async-start | bytes 393216 | tf_op jit(solution)/shard_map/psum | solution.py:11
  41.0 179.4 %reduce-scatter.3.cloned.1.call-start = ((), (), s32[]{:S(2)}) async-start(), calls=%async_computation.3 | async-start | bytes 73728 | tf_op jit(solution)/shard_map/reduce_scatter | solution.py:94
  41.2 0.7 copy-start.1
  42.5 0.7 copy-start.3
  44.2 0.7 copy-start.5
  46.1 0.7 copy-start.4
  114.0 25.1 %copy-start.2 = (f32[64,32]{0,1:T(8,128)S(1)}, f32[64,32]{0,1:T(8,128)}, u32[]{:S(2)}) copy-start(f32[64,32]{0,1:T(8,128)} %param.9) | copy-start | bytes 24580
  139.2 3.7 collective-permute-start
  142.9 3.8 collective-permute-start.1
  146.7 4.9 %collective-permute-start.2 = (bf16[64,128]{0,1:T(8,128)(2,1)S(1)}, bf16[64,128]{0,1:T(8,128)(2,1)S(1)}, u32[]{:S(2)}, u32[]{:S(2)}) collective-permute-start(bf16[64,128]{0,1:T(8,128)(2,1)S(1)} %maximum_select_fusion.2), channel_id=1, source_target_pairs={{0,4},{1,5},{2,6},{3,7},{4,0},{5,1},{6,2},{7,3},{8,12},{9,13},{10,... | collective-permute-start | bytes 49160 | tf_op jit(solution)/shard_map/ppermute | solution.py:79
  162.9 130.3 %all-reduce.12.cloned.1.call-start = ((), (), s32[]{:S(2)}) async-start(), calls=%async_computation.6 | async-start | bytes 262144 | tf_op jit(solution)/shard_map/psum | solution.py:11
  174.3 204.5 %reduce-scatter.5.cloned.1.call-start = ((), (), s32[]{:S(2)}) async-start(), calls=%async_computation.4 | async-start | bytes 73728 | tf_op jit(solution)/shard_map/reduce_scatter | solution.py:94
  294.0 3.7 collective-permute-start.3
  297.7 3.8 collective-permute-start.4
  301.5 4.9 %collective-permute-start.5 = (bf16[64,128]{0,1:T(8,128)(2,1)S(1)}, bf16[64,128]{0,1:T(8,128)(2,1)S(1)}, u32[]{:S(2)}, u32[]{:S(2)}) collective-permute-start(bf16[64,128]{0,1:T(8,128)(2,1)S(1)} %maximum_select_fusion.3), channel_id=1, source_target_pairs={{0,4},{1,5},{2,6},{3,7},{4,0},{5,1},{6,2},{7,3},{8,12},{9,13},{10,... | collective-permute-start | bytes 49160 | tf_op jit(solution)/shard_map/ppermute | solution.py:79
  317.7 133.3 %all-reduce.10.cloned.1.call-start = ((), (), s32[]{:S(2)}) async-start(), calls=%async_computation.5 | async-start | bytes 262144 | tf_op jit(solution)/shard_map/psum | solution.py:11
Sparse Core Ops, SparseCore 0:
  41.1 32.8 all-reduce.7
  163.0 57.3 reduce-scatter.2
  224.3 68.8 all-reduce.11
  317.8 60.9 reduce-scatter.4
  382.1 68.8 all-reduce.9
